TPU v7x, 32 devices: a whole 2x2x4 slice. The times are simulated.
32 devices in a mesh: grp: 2 (over x), cand: 8 (over z, y), seq: 2 (over core).
Axes of the slice: x: 2, y: 2, z: 4, core: 2. Of those that a mesh axis runs over, the one named last changes fastest.
Arguments:
- x_prefix: bfloat16 [8192, 2560], P(('grp', 'cand', 'seq')), parts along dimension 0, may hold values from -6 to 6
- b_prefix: bfloat16 [8192, 128], P(('grp', 'cand', 'seq')), parts along dimension 0, may hold values from -0.5 to 0.5
- code_prefix: int32 [8192, 40], P(('grp', 'cand', 'seq')), parts along dimension 0, may hold values from 0 to 500
- x_cand: bfloat16 [32, 512, 2560], P(('grp', 'cand'), None, 'seq'), parts along dimension 0, may hold values from -6 to 6
- b_cand: bfloat16 [32, 512, 128], P(('grp', 'cand')), parts along dimension 0, may hold values from -0.5 to 0.5
- c_cand: bfloat16 [32, 512, 128], P(('grp', 'cand')), parts along dimension 0, may hold values from -0.5 to 0.5
- code_cand: int32 [32, 512, 40], P(('grp', 'cand'), None, 'seq'), parts along dimension 0, may hold values from 0 to 500
- lengths: int32 [32], P(('grp', 'cand')), parts along dimension 0, may hold values from 1 to 2, as said below
- dy_cand: bfloat16 [32, 512, 2560], P(('grp', 'cand'), None, 'seq'), parts along dimension 0, may hold values from -1.5 to 1.5
Outputs:
- dx_prefix: bfloat16 [8192, 2560], P(('grp', 'cand', 'seq')), parts along dimension 0
- db_prefix: float32 [8192, 128], P(('grp', 'cand', 'seq')), parts along dimension 0
- dx_cand: bfloat16 [32, 512, 2560], P(('grp', 'cand'), None, 'seq'), parts along dimension 0
- db_cand: float32 [32, 512, 128], P(('grp', 'cand'), 'seq'), parts along dimension 0
- dc_cand: float32 [32, 512, 128], P(('grp', 'cand'), 'seq'), parts along dimension 0
There are 2 independent parts, one for each index of `grp`. A program takes and returns all parts, laid end to end along the dimension named above; each array names one. Nothing has to cross between parts.
Inputs may be any that keep to these rules, and one draw needn't show every extreme that they name: lengths count blocks of 256 tokens.
All inputs are finite; a program needn't handle non-finite values.
Results may differ from a plain program's by a relative error of at most 0.0015.
The roundings to bfloat16 on the way count: a program that leaves them out, or rounds other values in their place, can miss the bound.
Values may be sent and summed in bfloat16 or wider, within the bound.
No kernel may reach another device: no remote copies, remote signals or barrier semaphores. Data moves between devices by JAX's collectives and lax.ppermute only.
A program may use at most 256 MiB of HBM per device.

v0:
```python
import jax
import jax.numpy as jnp
from jax import lax
from jax.sharding import PartitionSpec as P

BLOCK = 256


def entering(shard, axis, combine, identity, reverse):
    length, mine = (lax.axis_size(axis), lax.axis_index(axis))
    everything = jax.tree.map(lambda part: lax.all_gather(part, axis), shard)
    start = jax.tree.map(
        lambda part, zero: jnp.broadcast_to(jnp.asarray(zero, part.dtype), part.shape),
        shard,
        identity,
    )

    def turn(k, before):
        at = length - 1 - k if reverse else k
        reached = at > mine if reverse else at < mine
        new = combine(before, jax.tree.map(lambda part: part[at], everything))
        return jax.tree.map(lambda a, b: jnp.where(reached, a, b), new, before)

    return lax.fori_loop(0, length, turn, start)


def broadcast(shard, axis, root):
    mine = lax.axis_index(axis) == root
    return lax.psum(jnp.where(mine, shard, jnp.zeros_like(shard)), axis)


def add_pair(earlier, later_part):
    return earlier + later_part


def link_states(earlier, later_part):
    return (
        earlier[0] * jnp.exp(later_part[1])[:, None, None] + later_part[0],
        earlier[1] + later_part[1],
    )


def candidate_terms(candidate, head_size):
    x_one, g_one, b_one, c_one, level_sum = candidate
    cand_len = x_one.shape[0]
    heads_total = level_sum.shape[1]
    position = jnp.arange(cand_len, dtype=jnp.int32)
    causal = position[:, None] >= position[None, :]
    scores = lax.dot_general(
        c_one, b_one, (((1,), (1,)), ((), ())), preferred_element_type=jnp.float32
    )

    def per_head(head_at, carry):
        weight_sum, grad_x = carry
        x_head = lax.dynamic_slice_in_dim(x_one, head_at * head_size, head_size, 1)
        g_head = lax.dynamic_slice_in_dim(g_one, head_at * head_size, head_size, 1)
        level_head = lax.dynamic_slice_in_dim(level_sum, head_at, 1, 1)[:, 0]
        decay_mat = jnp.where(
            causal, jnp.exp(level_head[:, None] - level_head[None, :]), jnp.zeros((), jnp.float32)
        )
        kernel = (scores * decay_mat).astype(jnp.bfloat16)
        dx_piece = lax.dot_general(
            kernel, g_head, (((0,), (0,)), ((), ())), preferred_element_type=jnp.float32
        )
        grad_x = lax.dynamic_update_slice_in_dim(
            grad_x, dx_piece.astype(jnp.bfloat16), head_at * head_size, 1
        )
        inner_prod = lax.dot_general(
            g_head, x_head, (((1,), (1,)), ((), ())), preferred_element_type=jnp.float32
        )
        return (weight_sum + inner_prod * decay_mat, grad_x)

    start = (jnp.zeros((cand_len, cand_len), jnp.float32), jnp.zeros_like(x_one))
    weight_sum, grad_x = lax.fori_loop(0, heads_total, per_head, start)
    db_part = jnp.dot(weight_sum.T, c_one.astype(jnp.float32), precision=lax.Precision.HIGHEST)
    dc_part = jnp.dot(weight_sum, b_one.astype(jnp.float32), precision=lax.Precision.HIGHEST)
    return (grad_x, db_part, dc_part)


def shards(x_prefix, b_prefix, code_prefix, x_cand, b_cand, c_cand, code_cand, lengths, dy_cand):
    pre_len, width = x_prefix.shape
    heads_total = code_prefix.shape[1]
    head_size = width // heads_total
    nstate = b_prefix.shape[1]
    cand_dev, cand_len, half_width = x_cand.shape
    half_heads = code_cand.shape[2]
    seq_at = lax.axis_index("seq")
    log_prefix = jnp.log1p(-code_prefix.astype(jnp.float32) * 1e-06)
    own_total = jnp.sum(log_prefix, axis=0)
    later_total = entering(own_total, ("cand", "seq"), add_pair, jnp.zeros_like(own_total), True)
    after_local = own_total[None, :] - jnp.cumsum(log_prefix, axis=0)
    weight = jnp.exp(after_local + later_total[None, :])
    weighted_b = (weight[:, :, None] * b_prefix[:, None, :].astype(jnp.float32)).astype(
        jnp.bfloat16
    )
    x_heads = x_prefix.reshape(pre_len, heads_total, head_size)
    state_full = jnp.einsum("jhp,jhn->hpn", x_heads, weighted_b, preferred_element_type=jnp.float32)
    own_state = state_full * jnp.exp(-later_total)[:, None, None]
    empty = (jnp.zeros_like(own_state), jnp.zeros_like(own_total))
    before = entering((own_state, own_total), ("cand", "seq"), link_states, empty, False)
    final_state = before[0] * jnp.exp(own_total)[:, None, None] + own_state
    root_last = lax.axis_size(("cand", "seq")) - 1
    whole_init = broadcast(final_state.astype(jnp.bfloat16), ("cand", "seq"), root_last)
    init_half = lax.dynamic_slice_in_dim(whole_init, seq_at * half_heads, half_heads, 0)
    position = jnp.arange(cand_len, dtype=jnp.int32)
    valid_rows = position[None, :] < lengths[:, None] * BLOCK
    g_cand = jnp.where(valid_rows[:, :, None], dy_cand, jnp.zeros_like(dy_cand))
    level_all = jnp.cumsum(jnp.log1p(-code_cand.astype(jnp.float32) * 1e-06), axis=1)

    def run_candidate(candidate):
        return candidate_terms(candidate, head_size)

    dx_cand, db_part, dc_part = lax.map(run_candidate, (x_cand, g_cand, b_cand, c_cand, level_all))
    amplitude = jnp.exp(level_all)
    g_heads = g_cand.reshape(cand_dev, cand_len, half_heads, head_size)
    decayed_g = (g_heads.astype(jnp.float32) * amplitude[:, :, :, None]).astype(jnp.bfloat16)
    dstate = jnp.einsum("cthp,ctn->hpn", decayed_g, c_cand, preferred_element_type=jnp.float32)
    dc_state = jnp.dot(
        decayed_g.reshape(cand_dev * cand_len, half_width),
        init_half.reshape(half_width, nstate),
        preferred_element_type=jnp.float32,
    )
    dc_total = dc_part + dc_state.reshape(cand_dev, cand_len, nstate)
    db_cand, dc_cand = (
        lax.psum_scatter(db_part, "seq", scatter_dimension=1, tiled=True),
        lax.psum_scatter(dc_total, "seq", scatter_dimension=1, tiled=True),
    )
    summed = lax.psum(dstate, "cand")
    grad_state = lax.all_gather(summed.astype(jnp.bfloat16), "seq", axis=0, tiled=True)
    dx_prefix = jnp.einsum(
        "jhn,hpn->jhp", weighted_b, grad_state, preferred_element_type=jnp.float32
    )
    dx_prefix = dx_prefix.astype(jnp.bfloat16).reshape(pre_len, width)
    projected = jnp.einsum("jhp,hpn->jhn", x_heads, grad_state, preferred_element_type=jnp.float32)
    db_prefix = jnp.sum(projected * weight[:, :, None], axis=1)
    return (dx_prefix, db_prefix, dx_cand, db_cand, dc_cand)


def solution(mesh):
    return jax.shard_map(
        shards,
        mesh=mesh,
        in_specs=(
            P(("grp", "cand", "seq"), None),
            P(("grp", "cand", "seq"), None),
            P(("grp", "cand", "seq"), None),
            P(("grp", "cand"), None, "seq"),
            P(("grp", "cand"), None, None),
            P(("grp", "cand"), None, None),
            P(("grp", "cand"), None, "seq"),
            P(("grp", "cand")),
            P(("grp", "cand"), None, "seq"),
        ),
        out_specs=(
            P(("grp", "cand", "seq"), None),
            P(("grp", "cand", "seq"), None),
            P(("grp", "cand"), None, "seq"),
            P(("grp", "cand"), "seq", None),
            P(("grp", "cand"), "seq", None),
        ),
        check_vma=False,
    )
```

profile of v0, /device:TPU:0, one launch (start us, length us, event | category | flops | bytes accessed | tf_op | source)
XLA Modules:
  0.0 392.8 jit_solution(4771028220192774179)
XLA Ops:
  11.1 34.9 %all-reduce = f32[640]{0:T(1024)S(1)} all-reduce(f32[640]{0:T(1024)S(1)} %dynamic-update-slice), channel_id=2, replica_groups=mesh['grp'=2,'cand'=8,'seq'=2] {'cand','seq'}, use_global_device_ids=true, to_apply=%add | all-reduce | flops 640 | bytes 5120
  47.9 1.6 copy.51
  49.6 2.1 fusion.40
  52.9 2.3 reduce-window.14
  55.7 4.6 %copy.43 = bf16[2,512,1280]{1,2,0:T(8,128)(2,1)} copy(bf16[2,512,1280]{2,1,0:T(8,128)(2,1)} %param.25) | data formatting | bytes 5242880 | tf_op args[8]
  60.4 5.0 %fusion.28 = (bf16[2,512,1280]{1,2,0:T(8,128)(2,1)}, bf16[2,512,1280]{1,2,0:T(8,128)(2,1)}) fusion(f32[2,512,20]{1,2,0:T(8,128)S(1)} %copy.46, bf16[2,512,1280]{1,2,0:T(8,128)(2,1)} %copy.43, pred[2,512]{1,0:T(4,128)(4,1)S(1)} %iota_compare_fusion.1), kind=kLoop, calls=%fused_computation.45 | loop fusion | flops 5242880 | bytes 7947264 | tf_op jit(solution)/shard_map/convert_element_type | solution.py:116
  65.4 92.7 %all-gather.4.cloned.1.call-done = f32[640,64,128]{2,1,0:T(8,128)} async-done(((f32[40,64,128]{2,1,0:T(8,128)}), f32[640,64,128]{2,1,0:T(8,128)}) %all-gather.4.cloned.1.call-update) | async-done | bytes 20971536 | tf_op jit(solution)/shard_map/all_gather | solution.py:11
  158.0 26.6 %while.63 = (s32[]{:T(128)}, f32[40,64,128]{2,1,0:T(8,128)S(1)}, s32[]{:T(128)}, f32[16,40]{1,0:T(8,128)S(1)}, f32[16,40,64,128]{3,2,1,0:T(8,128)}, /*index=5*/s32[]{:T(128)}, s32[]{:T(128)}) while((s32[]{:T(128)}, f32[40,64,128]{2,1,0:T(8,128)S(1)}, s32[]{:T(128)}, f32[16,40]{1,0:T(8,128)S(1)}, f32[16,40,64,128]{3,2,1,0:T(8,128)}, ...), condition=%wide.region_15.16_spmd.clone, body=%wide.region_14.15_spmd.clone.sunk | while | flops 1310724 | bytes 3932745 | solution.py:24
  158.1 1.7 fusion.82
  159.8 1.6 fusion.82
  161.5 1.6 fusion.82
  163.1 1.6 fusion.82
  164.8 1.6 fusion.82
  166.5 1.6 fusion.82
  168.1 1.6 fusion.82
  169.8 1.6 fusion.82
  171.4 1.6 fusion.82
  173.1 1.6 fusion.82
  174.8 1.6 fusion.82
  176.4 1.6 fusion.82
  178.1 1.6 fusion.82
  179.7 1.6 fusion.82
  181.4 1.6 fusion.82
  183.1 1.6 fusion.82
  185.9 144.2 %while.61 = (s32[]{:T(128)}, bf16[2,512,1280]{2,1,0:T(8,128)(2,1)}, f32[2,512,128]{2,1,0:T(8,128)}, f32[2,512,128]{2,1,0:T(8,128)}, bf16[2,512,1280]{2,1,0:T(8,1...) while((s32[]{:T(128)}, bf16[2,512,1280]{2,1,0:T(8,128)(2,1)}, ...), condition=%wide.region_12.13_spmd, body=%wide.region_9.12_spmd.sunk | while | flops 942440448 | bytes 26593764 | solution.py:113
  190.0 2.5 dynamic-slice_bitcast_fusion.2
  192.6 59.2 %while.64 = (s32[]{:T(128)}, f32[512,512]{1,0:T(8,128)S(1)}, bf16[512,1280]{0,1:T(8,128)(2,1)S(1)}, bf16[512,1280]{1,0:T(8,128)(2,1)}, bf16[512,1280]{1,0:T(8,12...) while((s32[]{:T(128)}, f32[512,512]{1,0:T(8,128)S(1)}, ...), condition=%wide.region_11.11_spmd.clone, body=%wide.region_10.10_spmd.clone.sunk | while | flops 70025224 | bytes 3619496 | solution.py:74
  192.7 1.6 fusion.86
  198.6 1.6 fusion.86
  207.5 1.6 fusion.86
  213.4 1.6 fusion.86
  216.4 1.6 fusion.86
  222.3 1.6 fusion.86
  231.2 1.6 fusion.86
  234.2 1.6 fusion.86
  243.1 1.6 fusion.86
  251.9 2.7 fusion.80
  262.2 2.5 dynamic-slice_bitcast_fusion.2
  264.8 59.2 %while.64 = (s32[]{:T(128)}, f32[512,512]{1,0:T(8,128)S(1)}, bf16[512,1280]{0,1:T(8,128)(2,1)S(1)}, bf16[512,1280]{1,0:T(8,128)(2,1)}, bf16[512,1280]{1,0:T(8,12...) while((s32[]{:T(128)}, f32[512,512]{1,0:T(8,128)S(1)}, ...), condition=%wide.region_11.11_spmd.clone, body=%wide.region_10.10_spmd.clone.sunk | while | flops 70025224 | bytes 3619496 | solution.py:74
  276.7 1.6 fusion.86
  288.5 1.6 fusion.86
  300.4 1.6 fusion.86
  324.0 2.7 fusion.80
  331.3 3.6 convolution_add_fusion
  334.9 1.8 fusion.41
  336.8 42.5 %all-reduce.5 = bf16[20,64,128]{2,1,0:T(8,128)(2,1)S(1)} all-reduce(f32[20,64,128]{2,1,0:T(8,128)S(1)} %fusion.41), channel_id=1, replica_groups=mesh['grp'=2,'cand'=8,'seq'=2] {'cand'}, use_global_device_ids=true, to_apply=%region_2.3 | all-reduce | flops 163840 | bytes 983040 | tf_op jit(solution)/shard_map/psum | solution.py:128
  379.3 2.3 all_gather.15
  382.1 1.6 copy.56
  (245 shorter events, 123.9 us)
Async XLA Ops:
  8.0 150.0 %all-gather.4.cloned.1.call-start = ((), (), s32[]{:S(2)}) async-start(), calls=%async_computation.5 | async-start | bytes 22282240 | tf_op jit(solution)/shard_map/all_gather | solution.py:11
  47.8 1.8 copy-start.13
  47.8 1.6 copy-start.12
  49.5 2.2 copy-start.2
  49.6 2.1 copy-start.9
  51.7 0.9 copy-start.11
  51.8 278.5 %all-reduce.4.cloned.1.call-start = ((), (), s32[]{:S(2)}) async-start(), calls=%async_computation.3 | async-start | bytes 1310720 | tf_op jit(solution)/shard_map/psum | solution.py:29
  55.7 4.7 %copy-start.7 = (f32[2,512,20]{1,2,0:T(8,128)}, f32[2,512,20]{1,2,0:T(8,128)S(1)}, u32[]{:S(2)}) copy-start(f32[2,512,20]{1,2,0:T(8,128)S(1)} %copy.46) | copy-start | bytes 245764
  55.7 4.6 %copy-start.15 = (s32[2]{0:T(128)S(1)}, s32[2]{0:T(128)}, u32[]{:S(2)}) copy-start(s32[2]{0:T(128)} %param.24) | copy-start | bytes 28
  158.0 26.7 %copy-start.1 = (f32[40,64,128]{2,1,0:T(8,128)S(1)}, f32[40,64,128]{2,1,0:T(8,128)}, u32[]{:S(2)}) copy-start(f32[40,64,128]{2,1,0:T(8,128)} %fusion.40) | copy-start | bytes 3932164
  185.8 199.5 %reduce-scatter.3.cloned.1.call-start = ((), (), s32[]{:S(2)}) async-start(), calls=%async_computation.2 | async-start | bytes 786432 | tf_op jit(solution)/shard_map/reduce_scatter | solution.py:125
  251.9 2.7 copy-start.4
  256.1 0.8 copy-start.5
  324.0 2.7 copy-start.4
  328.2 0.8 copy-start.5
  330.1 1.2 copy-start.6
  330.2 55.2 %reduce-scatter.5.cloned.1.call-start = ((), (), s32[]{:S(2)}) async-start(), calls=%async_computation.4 | async-start | bytes 786432 | tf_op jit(solution)/shard_map/reduce_scatter | solution.py:126
  331.3 3.6 copy-start
  331.3 3.6 copy-start.8
  336.7 44.9 %copy-start.10 = (f32[256,128]{0,1:T(8,128)S(1)}, f32[256,128]{0,1:T(8,128)}, u32[]{:S(2)}) copy-start(f32[256,128]{0,1:T(8,128)} %copy-done.9) | copy-start | bytes 393220
  336.7 44.8 %copy-start.14 = (f32[256,40]{0,1:T(8,128)S(1)}, f32[256,40]{0,1:T(8,128)}, u32[]{:S(2)}) copy-start(f32[256,40]{0,1:T(8,128)} %copy-done.13) | copy-start | bytes 122884
  382.1 1.6 copy-start.3
Sparse Core Ops, SparseCore 0:
  51.9 106.1 all-gather.3
  186.0 91.2 all-reduce.3
Sparse Core Ops, SparseCore 1:
  330.2 7.9 reduce-scatter.2
  341.0 9.0 reduce-scatter.4
where the time goes:
time: 396 us; the launch traced here: 393 us
  matrix products  136 us (34%)
  waiting for transfers between devices  92.8 us (23%)
  blocking collectives  79.7 us (20%)
  other arithmetic  36.7 us (9%)
  local copies, waits for them, and re-layouts  28.1 us (7%)
  between operations  16.5 us (4%)
    all_gather x1, waiting for transfers between devices, entering(): everything = jax.tree.map(lambda part: lax.all_gather(part, axis), shard)  92.7 us
    dot_general x40, matrix products, per_head(): lax.dot_general(g_head, x_head, (((1,), (1,)), ((), ())), preferred_eleme...  63 us
    dot_general x40, matrix products, per_head(): lax.dot_general(kernel, g_head, (((0,), (0,)), ((), ())), preferred_eleme...  53.1 us
    psum x1, blocking collectives, shards(): summed = lax.psum(dstate, 'cand')  42.5 us
    unnamed x1, blocking collectives  34.9 us
    select_n x32, other arithmetic, turn(): return jax.tree.map(lambda a, b: jnp.where(reached, a, b), new, before)  26.3 us
    unnamed x35, local copies, waits for them, and re-layouts  10.9 us
  transfers between devices with their start and end apart: 4, of which 1 were waited for; matrix products, arithmetic and copies ran while one was open for 42% of the time, Pallas kernels for 0%

commit v1 on v0

--- a/solution.py
+++ b/solution.py
@@ -125,7 +125,7 @@
         lax.psum_scatter(db_part, "seq", scatter_dimension=1, tiled=True),
         lax.psum_scatter(dc_total, "seq", scatter_dimension=1, tiled=True),
     )
-    summed = lax.psum(dstate, "cand")
+    summed = jnp.sum(lax.all_gather(dstate, "cand"), axis=0)
     grad_state = lax.all_gather(summed.astype(jnp.bfloat16), "seq", axis=0, tiled=True)
     dx_prefix = jnp.einsum(
         "jhn,hpn->jhp", weighted_b, grad_state, preferred_element_type=jnp.float32

time: 396 us -> 367 us (0.927)
  blocking collectives: 79.7 us -> 37.2 us
  waiting for transfers between devices: 92.8 us -> 108 us
    psum x1 -> x0, blocking collectives: 42.5 us -> none  [shards(): summed = lax.psum(dstate, 'cand')]
    all_gather x1, waiting for transfers between devices: 92.7 us -> 102 us  [entering(): everything = jax.tree.map(lambda part: lax.all_gather(part, axis), shard)]
    reduce_scatter x1, waiting for transfers between devices: 0.01 us -> 5.99 us  [shards(): lax.psum_scatter(dc_total, 'seq', scatter_dimension=1, tiled=True)]
    unnamed x35 -> x33, local copies, waits for them, and re-layouts: 10.9 us -> 10.9 us
  transfers between devices with their start and end apart: 4 -> 5, of which waited for: 1 -> 2; matrix products, arithmetic and copies ran while one was open for 42% -> 44% of each run, Pallas kernels for 0% -> 0%
where the time goes in v1:
time: 367 us; the launch traced here: 365 us
  matrix products  134 us (37%)
  waiting for transfers between devices  108 us (29%)
  other arithmetic  37.3 us (10%)
  blocking collectives  37.2 us (10%)
  local copies, waits for them, and re-layouts  28.1 us (8%)
  between operations  16.2 us (4%)
    all_gather x1, waiting for transfers between devices, entering(): everything = jax.tree.map(lambda part: lax.all_gather(part, axis), shard)  102 us
    dot_general x40, matrix products, per_head(): lax.dot_general(g_head, x_head, (((1,), (1,)), ((), ())), preferred_eleme...  63.1 us
    dot_general x40, matrix products, per_head(): lax.dot_general(kernel, g_head, (((0,), (0,)), ((), ())), preferred_eleme...  53.2 us
    unnamed x1, blocking collectives  34.9 us
    select_n x32, other arithmetic, turn(): return jax.tree.map(lambda a, b: jnp.where(reached, a, b), new, before)  26.3 us
    unnamed x33, local copies, waits for them, and re-layouts  10.9 us
  transfers between devices with their start and end apart: 5, of which 2 were waited for; matrix products, arithmetic and copies ran while one was open for 44% of the time, Pallas kernels for 0%

profile of v1, /device:TPU:0, one launch (start us, length us, event | category | flops | bytes accessed | tf_op | source)
XLA Modules:
  0.0 364.5 jit_solution(9388478137823456712)
XLA Ops:
  11.1 34.9 %all-reduce = f32[640]{0:T(1024)S(1)} all-reduce(f32[640]{0:T(1024)S(1)} %dynamic-update-slice), channel_id=3, replica_groups=mesh['grp'=2,'cand'=8,'seq'=2] {'cand','seq'}, use_global_device_ids=true, to_apply=%add | all-reduce | flops 640 | bytes 5120
  47.9 1.6 copy.51
  49.6 2.1 fusion.40
  52.9 2.3 reduce-window.14
  55.7 102.3 %all-gather.8.cloned.1.call-done = f32[640,64,128]{2,1,0:T(8,128)} async-done(((f32[40,64,128]{2,1,0:T(8,128)}), f32[640,64,128]{2,1,0:T(8,128)}) %all-gather.8.cloned.1.call-update) | async-done | bytes 20971536 | tf_op jit(solution)/shard_map/all_gather | solution.py:11
  158.0 26.6 %while.63 = (s32[]{:T(128)}, f32[40,64,128]{2,1,0:T(8,128)S(1)}, s32[]{:T(128)}, f32[16,40]{1,0:T(8,128)S(1)}, f32[16,40,64,128]{3,2,1,0:T(8,128)}, /*index=5*/s32[]{:T(128)}, s32[]{:T(128)}) while((s32[]{:T(128)}, f32[40,64,128]{2,1,0:T(8,128)S(1)}, s32[]{:T(128)}, f32[16,40]{1,0:T(8,128)S(1)}, f32[16,40,64,128]{3,2,1,0:T(8,128)}, ...), condition=%wide.region_15.16_spmd.clone, body=%wide.region_14.15_spmd.clone.sunk | while | flops 1310724 | bytes 3932745 | solution.py:24
  158.1 1.7 fusion.82
  159.8 1.6 fusion.82
  161.5 1.6 fusion.82
  163.1 1.6 fusion.82
  164.8 1.6 fusion.82
  166.5 1.6 fusion.82
  168.1 1.6 fusion.82
  169.8 1.6 fusion.82
  171.4 1.6 fusion.82
  173.1 1.6 fusion.82
  174.8 1.6 fusion.82
  176.4 1.6 fusion.82
  178.1 1.6 fusion.82
  179.7 1.6 fusion.82
  181.4 1.6 fusion.82
  183.1 1.6 fusion.82
  186.0 3.0 copy.43
  189.0 2.3 fusion.28
  192.9 1.7 fusion.41
  194.7 142.7 %while.61 = (s32[]{:T(128)}, bf16[2,512,1280]{2,1,0:T(8,128)(2,1)}, f32[2,512,128]{2,1,0:T(8,128)}, f32[2,512,128]{2,1,0:T(8,128)}, bf16[2,512,1280]{2,1,0:T(8,1...) while((s32[]{:T(128)}, bf16[2,512,1280]{2,1,0:T(8,128)(2,1)}, ...), condition=%wide.region_12.13_spmd, body=%wide.region_9.12_spmd.sunk | while | flops 942440448 | bytes 27642368 | solution.py:113
  198.8 2.5 dynamic-slice_bitcast_fusion.2
  201.5 59.4 %while.64 = (s32[]{:T(128)}, f32[512,512]{1,0:T(8,128)S(1)}, bf16[512,1280]{0,1:T(8,128)(2,1)S(1)}, bf16[512,1280]{1,0:T(8,128)(2,1)}, bf16[512,1280]{1,0:T(8,12...) while((s32[]{:T(128)}, f32[512,512]{1,0:T(8,128)S(1)}, ...), condition=%wide.region_11.11_spmd.clone, body=%wide.region_10.10_spmd.clone.sunk | while | flops 70025224 | bytes 3619496 | solution.py:74
  201.5 1.6 fusion.86
  204.5 1.6 fusion.86
  210.4 1.6 fusion.86
  213.4 1.6 fusion.86
  219.3 1.6 fusion.86
  225.3 1.6 fusion.86
  234.2 1.6 fusion.86
  252.0 1.6 fusion.86
  257.9 1.6 fusion.86
  260.9 2.7 fusion.80
  270.3 2.5 dynamic-slice_bitcast_fusion.2
  272.9 59.2 %while.64 = (s32[]{:T(128)}, f32[512,512]{1,0:T(8,128)S(1)}, bf16[512,1280]{0,1:T(8,128)(2,1)S(1)}, bf16[512,1280]{1,0:T(8,128)(2,1)}, bf16[512,1280]{1,0:T(8,12...) while((s32[]{:T(128)}, f32[512,512]{1,0:T(8,128)S(1)}, ...), condition=%wide.region_11.11_spmd.clone, body=%wide.region_10.10_spmd.clone.sunk | while | flops 70025224 | bytes 3619496 | solution.py:74
  272.9 1.6 fusion.86
  290.7 1.6 fusion.86
  332.1 2.7 fusion.80
  338.5 3.4 convolution_add_fusion
  342.0 3.3 reduce_sum.27
  345.3 2.3 all_gather.23
  348.1 1.6 copy.56
  351.4 6.0 %reduce-scatter.5.cloned.1.call-done = f32[2,256,128]{2,1,0:T(8,128)} async-done(((f32[2,512,128]{2,1,0:T(8,128)}), f32[2,256,128]{2,1,0:T(8,128)}) %reduce-scatter.5.cloned.1.call-update) | async-done | bytes 262160 | tf_op jit(solution)/shard_map/reduce_scatter | solution.py:126
  (250 shorter events, 125.4 us)
Async XLA Ops:
  8.0 150.0 %all-gather.8.cloned.1.call-start = ((), (), s32[]{:S(2)}) async-start(), calls=%async_computation.6 | async-start | bytes 22282240 | tf_op jit(solution)/shard_map/all_gather | solution.py:11
  47.8 1.8 copy-start.13
  47.8 1.6 copy-start.12
  49.5 2.2 copy-start.4
  49.6 2.1 copy-start.9
  51.7 0.9 copy-start.11
  51.7 3.9 %copy-start.15 = (s32[2]{0:T(128)S(1)}, s32[2]{0:T(128)}, u32[]{:S(2)}) copy-start(s32[2]{0:T(128)} %param.24) | copy-start | bytes 28
  51.8 285.7 %all-reduce.3.cloned.1.call-start = ((), (), s32[]{:S(2)}) async-start(), calls=%async_computation.3 | async-start | bytes 1310720 | tf_op jit(solution)/shard_map/psum | solution.py:29
  158.0 26.7 %copy-start.3 = (f32[40,64,128]{2,1,0:T(8,128)S(1)}, f32[40,64,128]{2,1,0:T(8,128)}, u32[]{:S(2)}) copy-start(f32[40,64,128]{2,1,0:T(8,128)} %fusion.40) | copy-start | bytes 3932164
  185.9 156.1 %all-gather.6.cloned.1.call-start = ((), (), s32[]{:S(2)}) async-start(), calls=%async_computation.5 | async-start | bytes 5898240 | tf_op jit(solution)/shard_map/all_gather | solution.py:128
  189.0 3.9 %copy-start.1 = (bf16[2,512,128]{2,1,0:T(8,128)(2,1)S(1)}, bf16[2,512,128]{2,1,0:T(8,128)(2,1)}, u32[]{:S(2)}) copy-start(bf16[2,512,128]{2,1,0:T(8,128)(2,1)} %param.22) | copy-start | bytes 786436
  191.3 1.6 copy-start
  194.6 156.8 %reduce-scatter.3.cloned.1.call-start = ((), (), s32[]{:S(2)}) async-start(), calls=%async_computation.2 | async-start | bytes 786432 | tf_op jit(solution)/shard_map/reduce_scatter | solution.py:125
  260.9 2.7 copy-start.2
  260.9 2.7 copy-start.6
  264.2 0.8 copy-start.7
  332.1 2.7 copy-start.2
  332.1 2.7 copy-start.6
  335.5 0.8 copy-start.7
  337.4 1.2 copy-start.8
  337.4 20.0 %reduce-scatter.5.cloned.1.call-start = ((), (), s32[]{:S(2)}) async-start(), calls=%async_computation.4 | async-start | bytes 786432 | tf_op jit(solution)/shard_map/reduce_scatter | solution.py:126
  342.0 5.6 %copy-start.10 = (f32[256,128]{0,1:T(8,128)S(1)}, f32[256,128]{0,1:T(8,128)}, u32[]{:S(2)}) copy-start(f32[256,128]{0,1:T(8,128)} %copy-done.9) | copy-start | bytes 393220
  342.0 5.6 %copy-start.14 = (f32[256,40]{0,1:T(8,128)S(1)}, f32[256,40]{0,1:T(8,128)}, u32[]{:S(2)}) copy-start(f32[256,40]{0,1:T(8,128)} %copy-done.13) | copy-start | bytes 122884
  348.1 1.6 copy-start.5
Sparse Core Ops, SparseCore 0:
  51.9 106.1 all-gather.7
  186.0 131.5 all-reduce.2
  337.5 7.9 reduce-scatter.2
  348.2 9.1 reduce-scatter.4
Sparse Core Ops, SparseCore 1:
  194.7 88.0 all-gather.5
